TPU v7x, 32 devices: a whole 2x2x4 slice. The times are simulated.
32 devices in a mesh: pipe: 2 (over core), dp: 8 (over z, x), tensor: 2 (over y).
Axes of the slice: x: 2, y: 2, z: 4, core: 2. Of those that a mesh axis runs over, the one named last changes fastest.
Arguments:
- normed_input: bfloat16 [2, 8, 1024, 4096], P('pipe', None, 'dp')
- key_grad: bfloat16 [2, 8, 1024, 512], P('pipe', None, 'dp', 'tensor')
- live_slots: int32 [2, 8], P('pipe'), may hold values from 0 to 1, as said below
- master: float32 [2, 4096, 512], P('pipe', 'dp', 'tensor'), may hold values from -4 to 4
- first_moment: float32 [2, 4096, 512], P('pipe', 'dp', 'tensor'), may hold values from -0.0009765625 to 0.0009765625
- second_moment: float32 [2, 4096, 512], P('pipe', 'dp', 'tensor'), as said below
Outputs:
- update: bfloat16 [2, 4096, 512], P('pipe', None, 'tensor')
Inputs may be any that keep to these rules, and one draw needn't show every extreme that they name: `live_slots`: in every draw exactly one section has all 8 slots live; every other section has at least one live and at least one dead slot. `second_moment`: every entry is positive.
All inputs are finite; a program needn't handle non-finite values.
Results may differ from a plain program's by a relative error of at most 0.0004.
Values may be sent and summed in bfloat16 or wider, within the bound.
No kernel may reach another device: no remote copies, remote signals or barrier semaphores. Data moves between devices by JAX's collectives and lax.ppermute only.
A program may use at most 64 MiB of HBM per device.

v0:
```python
import jax
import jax.numpy as jnp
from jax import lax
from jax.sharding import PartitionSpec as P

MOMENT_DECAY = 0.9
SQUARE_DECAY = 0.95
FIRST_CORRECTION = 1.0 - 0.9**20
SECOND_CORRECTION = 1.0 - 0.95**20
WEIGHT_DECAY = 0.1
CLIP_NORM = 1.0
EPSILON = 1e-08


def slot_term(inputs, key_grads, live_row, column_count):
    keep_mask = live_row.astype(key_grads.dtype)
    weighted = (key_grads * keep_mask[:, None, None]).reshape(-1, key_grads.shape[2])
    columns = inputs.reshape(-1, column_count)
    return lax.dot_general(
        columns, weighted, (((0,), (0,)), ((), ())), preferred_element_type=jnp.float32
    )


def butterfly_sum(value, axes):
    for axis in axes:
        size = lax.axis_size(axis)
        if size & size - 1:
            value = lax.psum(value, axis)
            continue
        bit = 1
        while bit < size:
            pairs = [(i, i ^ bit) for i in range(size)]
            value = value + lax.ppermute(value, axis, pairs)
            bit *= 2
    return value


def local(normed_input, key_grad, live_slots, master, first_moment, second_moment):
    inputs = normed_input[0]
    key_grads = key_grad[0]
    live_row = live_slots[0]
    live_count = jnp.sum(live_row)
    features = inputs.shape[2]
    summed = lax.psum_scatter(
        slot_term(inputs, key_grads, live_row, features), "dp", scatter_dimension=0, tiled=True
    )
    tokens_total = (live_count * (inputs.shape[1] * lax.axis_size("dp"))).astype(jnp.float32)
    grad_shard = summed / tokens_total
    squares = butterfly_sum(jnp.sum(grad_shard * grad_shard), ("pipe", "tensor", "dp"))
    clip_factor = jnp.minimum(1.0, CLIP_NORM / jnp.sqrt(squares))
    clipped = clip_factor * grad_shard
    moment1 = MOMENT_DECAY * first_moment[0] + (1.0 - MOMENT_DECAY) * clipped
    moment2 = SQUARE_DECAY * second_moment[0] + (1.0 - SQUARE_DECAY) * clipped * clipped
    update = (
        moment1 / FIRST_CORRECTION / (jnp.sqrt(moment2 / SECOND_CORRECTION) + EPSILON)
        + WEIGHT_DECAY * master[0]
    )
    update_rows = update.astype(jnp.bfloat16)[None]
    return lax.all_gather(update_rows, "dp", axis=1, tiled=True)


def solution(mesh):
    in_specs = (
        P("pipe", None, "dp", None),
        P("pipe", None, "dp", "tensor"),
        P("pipe", None),
        P("pipe", "dp", "tensor"),
        P("pipe", "dp", "tensor"),
        P("pipe", "dp", "tensor"),
    )
    out_specs = P("pipe", None, "tensor")
    return jax.shard_map(local, mesh=mesh, in_specs=in_specs, out_specs=out_specs, check_vma=False)
```

profile of v0, /device:TPU:0, one launch (start us, length us, event | category | flops | bytes accessed | tf_op | source)
XLA Modules:
  0.0 193.7 jit_solution(4177032211234704478)
XLA Ops:
  6.5 0.0 reduce-scatter.2.cloned.1.call-start
  6.5 1.4 fusion.16
  7.9 0.0 copy-start
  7.9 0.0 copy-start.1
  7.9 0.0 copy-start.2
  7.9 8.1 %fusion.2 = f32[4096,256]{0,1:T(8,128)} fusion(bf16[1,8,128,4096]{3,2,1,0:T(8,128)(2,1)} %param.6, bf16[1,8,128,256]{3,2,1,0:T(8,128)(2,1)} %param.7, bf16[8]{0:T(256)(128)(2,1)S(1)} %get-tuple-element.6), kind=kOutput, calls=%fused_computation.2 | convolution fusion | flops 2147745792 | bytes 13107216 | tf_op jit(solution)/shard_map/dot_general | solution.py:19
  16.0 0.0 reduce-scatter.2.cloned.1.call-update
  16.0 0.0 all-gather.3.cloned.1.call-start
  16.7 0.0 copy-done
  16.7 0.2 copy.10
  16.9 0.0 copy-done.1
  16.9 0.2 copy.7
  17.1 0.0 copy-done.2
  17.1 0.2 copy.9
  17.3 90.0 %reduce-scatter.2.cloned.1.call-done = f32[512,256]{0,1:T(8,128)} async-done(((f32[4096,256]{0,1:T(8,128)}), f32[512,256]{0,1:T(8,128)}) %reduce-scatter.2.cloned.1.call-update) | async-done | bytes 524304 | tf_op jit(solution)/shard_map/reduce_scatter | solution.py:44
  107.3 1.8 multiply_reduce_fusion
  109.1 0.0 collective-permute-start
  109.1 1.2 collective-permute-done
  111.7 2.8 %collective-permute-start.1 = (f32[]{:T(128)}, f32[]{:T(128)}, u32[]{:S(2)}, u32[]{:S(2)}) collective-permute-start(f32[]{:T(128)} %add.32), channel_id=1, source_target_pairs={{0,1},{1,0},{2,3},{3,2},{4,5},{5,4},{6,7},{7,6},{8,9},{9,8},{10,11... | collective-permute-start | bytes 20 | tf_op jit(solution)/shard_map/ppermute | solution.py:33
  114.5 0.7 collective-permute-done.1
  115.9 2.8 %collective-permute-start.2 = (f32[]{:T(128)}, f32[]{:T(128)}, u32[]{:S(2)}, u32[]{:S(2)}) collective-permute-start(f32[]{:T(128)} %add.33), channel_id=1, source_target_pairs={{0,2},{2,0},{4,6},{6,4},{8,10},{10,8},{12,14},{14,12},{1,3},{3,1},... | collective-permute-start | bytes 20 | tf_op jit(solution)/shard_map/ppermute | solution.py:33
  118.7 0.7 collective-permute-done.2
  120.2 3.0 %collective-permute-start.3 = (f32[]{:T(128)}, f32[]{:T(128)}, u32[]{:S(2)}, u32[]{:S(2)}) collective-permute-start(f32[]{:T(128)} %add.34), channel_id=1, source_target_pairs={{0,4},{2,6},{4,0},{6,2},{8,12},{10,14},{12,8},{14,10},{1,5},{3,7},... | collective-permute-start | bytes 20 | tf_op jit(solution)/shard_map/ppermute | solution.py:33
  123.2 0.5 collective-permute-done.3
  124.4 3.5 %collective-permute-start.4 = (f32[]{:T(128)}, f32[]{:T(128)}, u32[]{:S(2)}, u32[]{:S(2)}) collective-permute-start(f32[]{:T(128)} %add.35), channel_id=1, source_target_pairs={{0,8},{2,10},{4,12},{6,14},{8,0},{10,2},{12,4},{14,6},{1,9},{3,11}... | collective-permute-start | bytes 20 | tf_op jit(solution)/shard_map/ppermute | solution.py:33
  127.9 0.9 collective-permute-done.4
  129.6 2.2 %fusion.14 = bf16[512,256]{0,1:T(8,128)(2,1)} fusion(f32[1,512,256]{1,2,0:T(8,128)S(1)} %copy.10, f32[1,512,256]{1,2,0:T(8,128)S(1)} %copy.9, f32[1,512,256]{1,2,0:T(8,128)S(1)} %copy.7, f32[]{:T(128)S(6)} %min.3, f32[512,256]{0,1:T(8,128)} %reduce-scatter.2.cloned.1.call-done, f32[]{:T(128)S(6)} %convert_element_type.18), kind=kLoop, calls=%fused_computation.15 | loop fusion | flops 2097152 | bytes 2359304 | tf_op jit(solution)/shard_map/convert_element_type | solution.py:58
  131.8 0.0 all-gather.3.cloned.1.call-update
  131.8 51.0 %all-gather.3.cloned.1.call-done = bf16[4096,256]{0,1:T(8,128)(2,1)} async-done(((bf16[512,256]{0,1:T(8,128)(2,1)}), bf16[4096,256]{0,1:T(8,128)(2,1)}) %all-gather.3.cloned.1.call-update) | async-done | bytes 2097168 | tf_op jit(solution)/shard_map/all_gather | solution.py:59
  182.8 4.1 %copy.11 = bf16[1,4096,256]{2,1,0:T(8,128)(2,1)} copy(bf16[1,4096,256]{1,2,0:T(8,128)(2,1)} %bitcast.31) | data formatting | bytes 4194304 | tf_op jit(solution)/shard_map/all_gather | solution.py:59
Async XLA Ops:
  6.5 100.8 %reduce-scatter.2.cloned.1.call-start = ((), (), s32[]{:S(2)}) async-start(), calls=%async_computation.1 | async-start | bytes 4718592 | tf_op jit(solution)/shard_map/reduce_scatter | solution.py:44
  7.9 8.8 %copy-start = (f32[1,512,256]{2,1,0:T(8,128)S(1)}, f32[1,512,256]{2,1,0:T(8,128)}, u32[]{:S(2)}) copy-start(f32[1,512,256]{2,1,0:T(8,128)} %param.9) | copy-start | bytes 1572868
  7.9 9.0 %copy-start.1 = (f32[1,512,256]{2,1,0:T(8,128)S(1)}, f32[1,512,256]{2,1,0:T(8,128)}, u32[]{:S(2)}) copy-start(f32[1,512,256]{2,1,0:T(8,128)} %param.10) | copy-start | bytes 1572868
  7.9 9.2 %copy-start.2 = (f32[1,512,256]{2,1,0:T(8,128)S(1)}, f32[1,512,256]{2,1,0:T(8,128)}, u32[]{:S(2)}) copy-start(f32[1,512,256]{2,1,0:T(8,128)} %param.11) | copy-start | bytes 1572868
  16.0 166.8 %all-gather.3.cloned.1.call-start = ((), (), s32[]{:S(2)}) async-start(), calls=%async_computation.2 | async-start | bytes 2359296 | tf_op jit(solution)/shard_map/all_gather | solution.py:59
  109.1 1.2 collective-permute-start
  111.7 3.6 %collective-permute-start.1 = (f32[]{:T(128)}, f32[]{:T(128)}, u32[]{:S(2)}, u32[]{:S(2)}) collective-permute-start(f32[]{:T(128)} %add.32), channel_id=1, source_target_pairs={{0,1},{1,0},{2,3},{3,2},{4,5},{5,4},{6,7},{7,6},{8,9},{9,8},{10,11... | collective-permute-start | bytes 20 | tf_op jit(solution)/shard_map/ppermute | solution.py:33
  115.9 3.6 %collective-permute-start.2 = (f32[]{:T(128)}, f32[]{:T(128)}, u32[]{:S(2)}, u32[]{:S(2)}) collective-permute-start(f32[]{:T(128)} %add.33), channel_id=1, source_target_pairs={{0,2},{2,0},{4,6},{6,4},{8,10},{10,8},{12,14},{14,12},{1,3},{3,1},... | collective-permute-start | bytes 20 | tf_op jit(solution)/shard_map/ppermute | solution.py:33
  120.2 3.6 %collective-permute-start.3 = (f32[]{:T(128)}, f32[]{:T(128)}, u32[]{:S(2)}, u32[]{:S(2)}) collective-permute-start(f32[]{:T(128)} %add.34), channel_id=1, source_target_pairs={{0,4},{2,6},{4,0},{6,2},{8,12},{10,14},{12,8},{14,10},{1,5},{3,7},... | collective-permute-start | bytes 20 | tf_op jit(solution)/shard_map/ppermute | solution.py:33
  124.4 4.5 %collective-permute-start.4 = (f32[]{:T(128)}, f32[]{:T(128)}, u32[]{:S(2)}, u32[]{:S(2)}) collective-permute-start(f32[]{:T(128)} %add.35), channel_id=1, source_target_pairs={{0,8},{2,10},{4,12},{6,14},{8,0},{10,2},{12,4},{14,6},{1,9},{3,11}... | collective-permute-start | bytes 20 | tf_op jit(solution)/shard_map/ppermute | solution.py:33
Sparse Core Ops, SparseCore 0:
  16.1 91.1 reduce-scatter.1
  131.9 50.8 all-gather.2
where the time goes:
time: 194 us
  waiting for transfers between devices  145 us (75%)
  between operations  18.3 us (9%)
  starting transfers between devices  12.2 us (6%)
  matrix products  8.06 us (4%)
  other arithmetic  5.32 us (3%)
  local copies, waits for them, and re-layouts  4.66 us (2%)
    reduce_scatter x1, waiting for transfers between devices, local(): lax.psum_scatter(slot_term(inputs, key_grads, live_row, features), 'dp',...  90 us
    all_gather x1, waiting for transfers between devices, local(): return lax.all_gather(update_rows, 'dp', axis=1, tiled=True)  51 us
    ppermute x5, starting transfers between devices, butterfly_sum(): value = value + lax.ppermute(value, axis, pairs)  12.2 us
    dot_general x1, matrix products, slot_term(): lax.dot_general(columns, weighted, (((0,), (0,)), ((), ())), preferred_el...  8.06 us
    ppermute x5, waiting for transfers between devices, butterfly_sum(): value = value + lax.ppermute(value, axis, pairs)  4.16 us
    all_gather x1, local copies, waits for them, and re-layouts, local(): return lax.all_gather(update_rows, 'dp', axis=1, tiled=True)  4.06 us
  transfers between devices with their start and end apart: 7, of which 7 were waited for; matrix products, arithmetic and copies ran while one was open for 0% of the time, Pallas kernels for 0%

commit v1 on v0

--- a/solution.py
+++ b/solution.py
@@ -10,6 +10,19 @@
 WEIGHT_DECAY = 0.1
 CLIP_NORM = 1.0
 EPSILON = 1e-08
+
+
+def ring_gather(value, axis, dim):
+    ways = lax.axis_size(axis)
+    up = [(d, (d + 1) % ways) for d in range(ways)]
+    down = [(d, (d - 1) % ways) for d in range(ways)]
+    earlier, later = ([value], [value])
+    for _ in range(ways // 2):
+        earlier.append(lax.ppermute(earlier[-1], axis, up))
+    for _ in range((ways - 1) // 2):
+        later.append(lax.ppermute(later[-1], axis, down))
+    line = jnp.concatenate([*earlier[::-1], *later[1:]], axis=dim)
+    return jnp.roll(line, (lax.axis_index(axis) - ways // 2) * value.shape[dim], axis=dim)
 
 
 def slot_term(inputs, key_grads, live_row, column_count):
@@ -56,7 +69,7 @@
         + WEIGHT_DECAY * master[0]
     )
     update_rows = update.astype(jnp.bfloat16)[None]
-    return lax.all_gather(update_rows, "dp", axis=1, tiled=True)
+    return ring_gather(update_rows, "dp", 1)
 
 
 def solution(mesh):

time: 194 us -> 192 us (0.990)
  waiting for transfers between devices: 145 us -> 129 us
  starting transfers between devices: 12.2 us -> 27.4 us
    all_gather x1 -> x0, waiting for transfers between devices: 51 us -> none  [local(): return lax.all_gather(update_rows, 'dp', axis=1, tiled=True)]
    ppermute x0 -> x7, waiting for transfers between devices: none -> 34.8 us  [the longest x4 31.8 us: ring_gather(): earlier.append(lax.ppermute(earlier[-1], axis, up))]
    ppermute x0 -> x7, starting transfers between devices: none -> 15.2 us  [the longest x4 8.95 us: ring_gather(): earlier.append(lax.ppermute(earlier[-1], axis, up))]
    all_gather x1 -> x0, local copies, waits for them, and re-layouts: 4.06 us -> none  [local(): return lax.all_gather(update_rows, 'dp', axis=1, tiled=True)]
    dynamic_slice x0 -> x2, local copies, waits for them, and re-layouts: none -> 2.6 us  [ring_gather(): jnp.roll(line, (lax.axis_index(axis) - ways // 2) * value.shape[dim], axi...]
    convert_element_type x1 -> x0, other arithmetic: 2.17 us -> none  [local(): update_rows = update.astype(jnp.bfloat16)[None]]
  transfers between devices with their start and end apart: 7 -> 13, of which waited for: 7 -> 13; matrix products, arithmetic and copies ran while one was open for 0% -> 0% of each run, Pallas kernels for 0% -> 0%
where the time goes in v1:
time: 192 us; the launch traced here: 191 us
  waiting for transfers between devices  129 us (67%)
  starting transfers between devices  27.4 us (14%)
  between operations  18.2 us (9%)
  matrix products  7.97 us (4%)
  other arithmetic  4.62 us (2%)
  local copies, waits for them, and re-layouts  3.89 us (2%)
    reduce_scatter x1, waiting for transfers between devices, local(): lax.psum_scatter(slot_term(inputs, key_grads, live_row, features), 'dp',...  89.7 us
    ppermute x4, waiting for transfers between devices, ring_gather(): earlier.append(lax.ppermute(earlier[-1], axis, up))  31.8 us
    ppermute x5, starting transfers between devices, butterfly_sum(): value = value + lax.ppermute(value, axis, pairs)  12.2 us
    ppermute x4, starting transfers between devices, ring_gather(): earlier.append(lax.ppermute(earlier[-1], axis, up))  8.95 us
    dot_general x1, matrix products, slot_term(): lax.dot_general(columns, weighted, (((0,), (0,)), ((), ())), preferred_el...  7.97 us
    ppermute x3, starting transfers between devices, ring_gather(): later.append(lax.ppermute(later[-1], axis, down))  6.21 us
    ppermute x5, waiting for transfers between devices, butterfly_sum(): value = value + lax.ppermute(value, axis, pairs)  4.9 us
  transfers between devices with their start and end apart: 13, of which 13 were waited for; matrix products, arithmetic and copies ran while one was open for 0% of the time, Pallas kernels for 0%

profile of v1, /device:TPU:0, one launch (start us, length us, event | category | flops | bytes accessed | tf_op | source)
XLA Modules:
  0.0 191.4 jit_solution(2471832799578423677)
XLA Ops:
  6.5 1.4 fusion.17
  7.9 8.0 %fusion.2 = f32[4096,256]{0,1:T(8,128)} fusion(bf16[1,8,128,4096]{3,2,1,0:T(8,128)(2,1)} %param.6, bf16[1,8,128,256]{3,2,1,0:T(8,128)(2,1)} %param.7, bf16[8]{0:T(256)(128)(2,1)S(1)} %get-tuple-element.6), kind=kOutput, calls=%fused_computation.2 | convolution fusion | flops 2147745792 | bytes 13107216 | tf_op jit(solution)/shard_map/dot_general | solution.py:32
  16.7 0.3 copy-done
  17.1 0.2 copy.7
  17.4 0.2 copy.9
  17.6 89.7 %reduce-scatter.2.cloned.1.call-done = f32[512,256]{0,1:T(8,128)} async-done(((f32[4096,256]{0,1:T(8,128)}), f32[512,256]{0,1:T(8,128)}) %reduce-scatter.2.cloned.1.call-update) | async-done | bytes 524304 | tf_op jit(solution)/shard_map/reduce_scatter | solution.py:57
  107.2 1.8 multiply_reduce_fusion
  109.0 1.4 collective-permute-done
  111.7 2.8 %collective-permute-start.1 = (f32[]{:T(128)}, f32[]{:T(128)}, u32[]{:S(2)}, u32[]{:S(2)}) collective-permute-start(f32[]{:T(128)} %add.43), channel_id=1, source_target_pairs={{0,1},{1,0},{2,3},{3,2},{4,5},{5,4},{6,7},{7,6},{8,9},{9,8},{10,11... | collective-permute-start | bytes 20 | tf_op jit(solution)/shard_map/ppermute | solution.py:46
  114.5 0.9 collective-permute-done.1
  116.0 2.8 %collective-permute-start.2 = (f32[]{:T(128)}, f32[]{:T(128)}, u32[]{:S(2)}, u32[]{:S(2)}) collective-permute-start(f32[]{:T(128)} %add.44), channel_id=1, source_target_pairs={{0,2},{2,0},{4,6},{6,4},{8,10},{10,8},{12,14},{14,12},{1,3},{3,1},... | collective-permute-start | bytes 20 | tf_op jit(solution)/shard_map/ppermute | solution.py:46
  118.8 0.9 collective-permute-done.2
  120.4 3.1 %collective-permute-start.3 = (f32[]{:T(128)}, f32[]{:T(128)}, u32[]{:S(2)}, u32[]{:S(2)}) collective-permute-start(f32[]{:T(128)} %add.45), channel_id=1, source_target_pairs={{0,4},{2,6},{4,0},{6,2},{8,12},{10,14},{12,8},{14,10},{1,5},{3,7},... | collective-permute-start | bytes 20 | tf_op jit(solution)/shard_map/ppermute | solution.py:46
  123.4 0.6 collective-permute-done.3
  124.7 3.5 %collective-permute-start.4 = (f32[]{:T(128)}, f32[]{:T(128)}, u32[]{:S(2)}, u32[]{:S(2)}) collective-permute-start(f32[]{:T(128)} %add.46), channel_id=1, source_target_pairs={{0,8},{2,10},{4,12},{6,14},{8,0},{10,2},{12,4},{14,6},{1,9},{3,11}... | collective-permute-start | bytes 20 | tf_op jit(solution)/shard_map/ppermute | solution.py:46
  128.2 1.1 collective-permute-done.4
  130.0 1.5 fusion.16
  131.5 1.5 collective-permute-start.5
  133.0 8.8 %collective-permute-done.5 = bf16[1,512,256]{1,2,0:T(8,128)(2,1)S(1)} collective-permute-done((bf16[1,512,256]{1,2,0:T(8,128)(2,1)S(1)}, bf16[1,512,256]{1,2,0:T(8,128)(2,1)S(1)}, u32[]{:S(2)}, u32[]{:S(2)}) %collective-permute-start.5) | collective-permute-done | bytes 262176 | tf_op jit(solution)/shard_map/ppermute | solution.py:21
  141.8 2.5 %collective-permute-start.6 = (bf16[1,512,256]{1,2,0:T(8,128)(2,1)S(1)}, bf16[1,512,256]{1,2,0:T(8,128)(2,1)S(1)}, u32[]{:S(2)}, u32[]{:S(2)}) collective-permute-start(bf16[1,512,256]{1,2,0:T(8,128)(2,1)S(1)} %collective-permute-done.5), channel_id=1, source_target_pairs={{0,2},{2,4},{4,6},{6,8},{8,10},{10,12},{12,14},{14,0},{1,3},{3,5},... | collective-permute-start | bytes 786440 | tf_op jit(solution)/shard_map/ppermute | solution.py:21
  144.2 2.2 %collective-permute-start.9 = (bf16[1,512,256]{1,2,0:T(8,128)(2,1)S(1)}, bf16[1,512,256]{1,2,0:T(8,128)(2,1)S(1)}, u32[]{:S(2)}, u32[]{:S(2)}) collective-permute-start(bf16[1,512,256]{1,2,0:T(8,128)(2,1)S(1)} %fusion.16), channel_id=1, source_target_pairs={{0,14},{2,0},{4,2},{6,4},{8,6},{10,8},{12,10},{14,12},{1,15},{3,1}... | collective-permute-start | bytes 786440 | tf_op jit(solution)/shard_map/ppermute | solution.py:23
  146.5 9.7 %collective-permute-done.6 = bf16[1,512,256]{1,2,0:T(8,128)(2,1)S(1)} collective-permute-done((bf16[1,512,256]{1,2,0:T(8,128)(2,1)S(1)}, bf16[1,512,256]{1,2,0:T(8,128)(2,1)S(1)}, u32[]{:S(2)}, u32[]{:S(2)}) %collective-permute-start.6) | collective-permute-done | bytes 262176 | tf_op jit(solution)/shard_map/ppermute | solution.py:21
  156.2 2.5 %collective-permute-start.7 = (bf16[1,512,256]{1,2,0:T(8,128)(2,1)S(1)}, bf16[1,512,256]{1,2,0:T(8,128)(2,1)S(1)}, u32[]{:S(2)}, u32[]{:S(2)}) collective-permute-start(bf16[1,512,256]{1,2,0:T(8,128)(2,1)S(1)} %collective-permute-done.6), channel_id=1, source_target_pairs={{0,2},{2,4},{4,6},{6,8},{8,10},{10,12},{12,14},{14,0},{1,3},{3,5},... | collective-permute-start | bytes 786440 | tf_op jit(solution)/shard_map/ppermute | solution.py:21
  158.6 0.3 collective-permute-done.9
  158.9 1.9 %collective-permute-start.10 = (bf16[1,512,256]{1,2,0:T(8,128)(2,1)S(1)}, bf16[1,512,256]{1,2,0:T(8,128)(2,1)S(1)}, u32[]{:S(2)}, u32[]{:S(2)}) collective-permute-start(bf16[1,512,256]{1,2,0:T(8,128)(2,1)S(1)} %collective-permute-done.9), channel_id=1, source_target_pairs={{0,14},{2,0},{4,2},{6,4},{8,6},{10,8},{12,10},{14,12},{1,15},{3,1}... | collective-permute-start | bytes 786440 | tf_op jit(solution)/shard_map/ppermute | solution.py:23
  160.9 8.9 %collective-permute-done.7 = bf16[1,512,256]{1,2,0:T(8,128)(2,1)S(1)} collective-permute-done((bf16[1,512,256]{1,2,0:T(8,128)(2,1)S(1)}, bf16[1,512,256]{1,2,0:T(8,128)(2,1)S(1)}, u32[]{:S(2)}, u32[]{:S(2)}) %collective-permute-start.7) | collective-permute-done | bytes 262176 | tf_op jit(solution)/shard_map/ppermute | solution.py:21
  169.8 2.5 %collective-permute-start.8 = (bf16[1,512,256]{1,2,0:T(8,128)(2,1)S(1)}, bf16[1,512,256]{1,2,0:T(8,128)(2,1)S(1)}, u32[]{:S(2)}, u32[]{:S(2)}) collective-permute-start(bf16[1,512,256]{1,2,0:T(8,128)(2,1)S(1)} %collective-permute-done.7), channel_id=1, source_target_pairs={{0,2},{2,4},{4,6},{6,8},{8,10},{10,12},{12,14},{14,0},{1,3},{3,5},... | collective-permute-start | bytes 786440 | tf_op jit(solution)/shard_map/ppermute | solution.py:21
  172.3 0.2 collective-permute-done.10
  172.5 2.0 %collective-permute-start.11 = (bf16[1,512,256]{1,2,0:T(8,128)(2,1)S(1)}, bf16[1,512,256]{1,2,0:T(8,128)(2,1)S(1)}, u32[]{:S(2)}, u32[]{:S(2)}) collective-permute-start(bf16[1,512,256]{1,2,0:T(8,128)(2,1)S(1)} %collective-permute-done.10), channel_id=1, source_target_pairs={{0,14},{2,0},{4,2},{6,4},{8,6},{10,8},{12,10},{14,12},{1,15},{3,1}... | collective-permute-start | bytes 786440 | tf_op jit(solution)/shard_map/ppermute | solution.py:23
  174.5 4.5 %collective-permute-done.8 = bf16[1,512,256]{1,2,0:T(8,128)(2,1)S(1)} collective-permute-done((bf16[1,512,256]{1,2,0:T(8,128)(2,1)S(1)}, bf16[1,512,256]{1,2,0:T(8,128)(2,1)S(1)}, u32[]{:S(2)}, u32[]{:S(2)}) %collective-permute-start.8) | collective-permute-done | bytes 262176 | tf_op jit(solution)/shard_map/ppermute | solution.py:21
  179.2 2.5 %collective-permute-done.11 = bf16[1,512,256]{1,2,0:T(8,128)(2,1)S(1)} collective-permute-done((bf16[1,512,256]{1,2,0:T(8,128)(2,1)S(1)}, bf16[1,512,256]{1,2,0:T(8,128)(2,1)S(1)}, u32[]{:S(2)}, u32[]{:S(2)}) %collective-permute-start.11) | collective-permute-done | bytes 262176 | tf_op jit(solution)/shard_map/ppermute | solution.py:23
  182.1 2.5 %copy.11 = bf16[1,4096,256]{2,1,0:T(8,128)(2,1)} copy(bf16[1,4096,256]{1,2,0:T(8,128)(2,1)S(1)} %constant_dynamic-slice_fusion) | data formatting | bytes 4194304 | tf_op jit(solution)/shard_map/jit(_roll_dynamic)/dynamic_slice | solution.py:25
  (26 shorter events, 0.8 us)
Async XLA Ops:
  6.5 100.7 %reduce-scatter.2.cloned.1.call-start = ((), (), s32[]{:S(2)}) async-start(), calls=%async_computation.1 | async-start | bytes 4718592 | tf_op jit(solution)/shard_map/reduce_scatter | solution.py:57
  15.9 1.1 copy-start
  15.9 1.3 copy-start.1
  15.9 1.5 copy-start.2
  109.0 1.4 collective-permute-start
  111.7 3.7 %collective-permute-start.1 = (f32[]{:T(128)}, f32[]{:T(128)}, u32[]{:S(2)}, u32[]{:S(2)}) collective-permute-start(f32[]{:T(128)} %add.43), channel_id=1, source_target_pairs={{0,1},{1,0},{2,3},{3,2},{4,5},{5,4},{6,7},{7,6},{8,9},{9,8},{10,11... | collective-permute-start | bytes 20 | tf_op jit(solution)/shard_map/ppermute | solution.py:46
  116.0 3.7 %collective-permute-start.2 = (f32[]{:T(128)}, f32[]{:T(128)}, u32[]{:S(2)}, u32[]{:S(2)}) collective-permute-start(f32[]{:T(128)} %add.44), channel_id=1, source_target_pairs={{0,2},{2,0},{4,6},{6,4},{8,10},{10,8},{12,14},{14,12},{1,3},{3,1},... | collective-permute-start | bytes 20 | tf_op jit(solution)/shard_map/ppermute | solution.py:46
  120.4 3.7 %collective-permute-start.3 = (f32[]{:T(128)}, f32[]{:T(128)}, u32[]{:S(2)}, u32[]{:S(2)}) collective-permute-start(f32[]{:T(128)} %add.45), channel_id=1, source_target_pairs={{0,4},{2,6},{4,0},{6,2},{8,12},{10,14},{12,8},{14,10},{1,5},{3,7},... | collective-permute-start | bytes 20 | tf_op jit(solution)/shard_map/ppermute | solution.py:46
  124.7 4.6 %collective-permute-start.4 = (f32[]{:T(128)}, f32[]{:T(128)}, u32[]{:S(2)}, u32[]{:S(2)}) collective-permute-start(f32[]{:T(128)} %add.46), channel_id=1, source_target_pairs={{0,8},{2,10},{4,12},{6,14},{8,0},{10,2},{12,4},{14,6},{1,9},{3,11}... | collective-permute-start | bytes 20 | tf_op jit(solution)/shard_map/ppermute | solution.py:46
  131.5 10.3 %collective-permute-start.5 = (bf16[1,512,256]{1,2,0:T(8,128)(2,1)S(1)}, bf16[1,512,256]{1,2,0:T(8,128)(2,1)S(1)}, u32[]{:S(2)}, u32[]{:S(2)}) collective-permute-start(bf16[1,512,256]{1,2,0:T(8,128)(2,1)S(1)} %fusion.16), channel_id=1, source_target_pairs={{0,2},{2,4},{4,6},{6,8},{8,10},{10,12},{12,14},{14,0},{1,3},{3,5},... | collective-permute-start | bytes 786440 | tf_op jit(solution)/shard_map/ppermute | solution.py:21
  141.8 14.4 %collective-permute-start.6 = (bf16[1,512,256]{1,2,0:T(8,128)(2,1)S(1)}, bf16[1,512,256]{1,2,0:T(8,128)(2,1)S(1)}, u32[]{:S(2)}, u32[]{:S(2)}) collective-permute-start(bf16[1,512,256]{1,2,0:T(8,128)(2,1)S(1)} %collective-permute-done.5), channel_id=1, source_target_pairs={{0,2},{2,4},{4,6},{6,8},{8,10},{10,12},{12,14},{14,0},{1,3},{3,5},... | collective-permute-start | bytes 786440 | tf_op jit(solution)/shard_map/ppermute | solution.py:21
  144.2 14.7 %collective-permute-start.9 = (bf16[1,512,256]{1,2,0:T(8,128)(2,1)S(1)}, bf16[1,512,256]{1,2,0:T(8,128)(2,1)S(1)}, u32[]{:S(2)}, u32[]{:S(2)}) collective-permute-start(bf16[1,512,256]{1,2,0:T(8,128)(2,1)S(1)} %fusion.16), channel_id=1, source_target_pairs={{0,14},{2,0},{4,2},{6,4},{8,6},{10,8},{12,10},{14,12},{1,15},{3,1}... | collective-permute-start | bytes 786440 | tf_op jit(solution)/shard_map/ppermute | solution.py:23
  156.2 13.6 %collective-permute-start.7 = (bf16[1,512,256]{1,2,0:T(8,128)(2,1)S(1)}, bf16[1,512,256]{1,2,0:T(8,128)(2,1)S(1)}, u32[]{:S(2)}, u32[]{:S(2)}) collective-permute-start(bf16[1,512,256]{1,2,0:T(8,128)(2,1)S(1)} %collective-permute-done.6), channel_id=1, source_target_pairs={{0,2},{2,4},{4,6},{6,8},{8,10},{10,12},{12,14},{14,0},{1,3},{3,5},... | collective-permute-start | bytes 786440 | tf_op jit(solution)/shard_map/ppermute | solution.py:21
  158.9 13.5 %collective-permute-start.10 = (bf16[1,512,256]{1,2,0:T(8,128)(2,1)S(1)}, bf16[1,512,256]{1,2,0:T(8,128)(2,1)S(1)}, u32[]{:S(2)}, u32[]{:S(2)}) collective-permute-start(bf16[1,512,256]{1,2,0:T(8,128)(2,1)S(1)} %collective-permute-done.9), channel_id=1, source_target_pairs={{0,14},{2,0},{4,2},{6,4},{8,6},{10,8},{12,10},{14,12},{1,15},{3,1}... | collective-permute-start | bytes 786440 | tf_op jit(solution)/shard_map/ppermute | solution.py:23
  169.8 9.2 %collective-permute-start.8 = (bf16[1,512,256]{1,2,0:T(8,128)(2,1)S(1)}, bf16[1,512,256]{1,2,0:T(8,128)(2,1)S(1)}, u32[]{:S(2)}, u32[]{:S(2)}) collective-permute-start(bf16[1,512,256]{1,2,0:T(8,128)(2,1)S(1)} %collective-permute-done.7), channel_id=1, source_target_pairs={{0,2},{2,4},{4,6},{6,8},{8,10},{10,12},{12,14},{14,0},{1,3},{3,5},... | collective-permute-start | bytes 786440 | tf_op jit(solution)/shard_map/ppermute | solution.py:21
  172.5 9.2 %collective-permute-start.11 = (bf16[1,512,256]{1,2,0:T(8,128)(2,1)S(1)}, bf16[1,512,256]{1,2,0:T(8,128)(2,1)S(1)}, u32[]{:S(2)}, u32[]{:S(2)}) collective-permute-start(bf16[1,512,256]{1,2,0:T(8,128)(2,1)S(1)} %collective-permute-done.10), channel_id=1, source_target_pairs={{0,14},{2,0},{4,2},{6,4},{8,6},{10,8},{12,10},{14,12},{1,15},{3,1}... | collective-permute-start | bytes 786440 | tf_op jit(solution)/shard_map/ppermute | solution.py:23
Sparse Core Ops, SparseCore 0:
  16.0 91.1 reduce-scatter.1
